TPU v7x, 512 devices: a whole 4x8x8 slice. The times are simulated.
512 devices in a mesh: req: 128 (over z, y, core), grp: 4 (over x).
Axes of the slice: x: 4, y: 8, z: 8, core: 2. Of those that a mesh axis runs over, the one named last changes fastest.
Arguments:
- owner_slab: bfloat16 [65536, 1024], P('req'), may hold values from -6 to 6
- segment_ids: int32 [128, 512], P('req'), may hold values from 0 to 511, as said below
- head_weights: bfloat16 [1024, 16, 192], P(None, 'grp')
- merge_weights: bfloat16 [16, 64, 1024], P('grp'), may hold values from -0.1875 to 0.1875
- first_gain: float32 [1024], replicated, may hold values from 0.25 to 1.75
- first_bias: float32 [1024], replicated, may hold values from -3 to 3
- up_weights: bfloat16 [1024, 4096], P('req', 'grp'), may hold values from -0.1875 to 0.1875
- down_weights: bfloat16 [4096, 1024], P('grp', 'req'), may hold values from -0.09375 to 0.09375
- second_gain: float32 [1024], replicated, may hold values from 0.25 to 1.75
- second_bias: float32 [1024], replicated, may hold values from -3 to 3
- page_table: int32 [128, 4], P('req'), may hold values from 0 to 3, each once within a row
- row_map: int32 [128, 4, 128], P('req', 'grp'), may hold values from 0 to 127, each once within a row
Outputs:
- layer_out: bfloat16 [65536, 1024], P(('req', 'grp'))
- cache_pages: bfloat16 [512, 128, 16, 128], P('req', None, 'grp')
Inputs may be any that keep to these rules, and one draw needn't show every extreme that they name: `segment_ids`: within each slab the ids start at 0, never fall and rise by at most one from row to row; in one slab all 512 rows form a single request, and in one other slab every row is a request of its own.
All inputs are finite; a program needn't handle non-finite values.
Results may differ from a plain program's by a relative error of at most 0.0075.
Values may be sent and summed in bfloat16 or wider, within the bound.
No kernel may reach another device: no remote copies, remote signals or barrier semaphores. Data moves between devices by JAX's collectives and lax.ppermute only.
A program may use at most 64 MiB of HBM per device.

v0:
```python
import math
import jax
import jax.numpy as jnp
import numpy as np
from jax import lax
from jax.sharding import Mesh
from jax.sharding import PartitionSpec as P

EPSILON = 1e-05
REQ = ("rz", "ry", "rc")


def layer_norm(values, gain, bias):
    center = values - jnp.mean(values, axis=-1, keepdims=True)
    spread = jnp.mean(center * center, axis=-1, keepdims=True)
    return center * lax.rsqrt(spread + EPSILON) * gain + bias


def split_req(mesh):
    column = mesh.devices[:, 0]
    try:
        cores = len({d.core_on_chip for d in column})
        ys = len({d.coords[1] for d in column})
        zs = len({d.coords[2] for d in column})
    except AttributeError:
        return (column.shape[0], 1, 1)
    if zs * ys * cores != column.shape[0]:
        return (column.shape[0], 1, 1)
    return (zs, ys, cores)


def gather_rows(block, first, second):
    a = lax.all_gather(block, first, axis=0, tiled=False)
    b = lax.all_gather(a, second, axis=0, tiled=False)
    c = lax.all_gather(b, "rc", axis=0, tiled=False)
    if first == "ry":
        c = jnp.transpose(c, (1, 2, 0, 3, 4))
    else:
        c = jnp.transpose(c, (2, 1, 0, 3, 4))
    return c.reshape(-1, block.shape[1])


def local(
    owner_slab,
    segment_ids,
    head_weights,
    merge_weights,
    first_gain,
    first_bias,
    up_weights,
    down_weights,
    second_gain,
    second_bias,
    page_table,
    row_map,
):
    group = lax.axis_size("grp")
    owners = lax.axis_size(REQ)
    zs = lax.axis_size("rz")
    rows_all = owner_slab.shape[0]
    width = owner_slab.shape[1]
    quarter = rows_all // group
    local_heads = head_weights.shape[1]
    head_dim = head_weights.shape[2] // 3
    up_full = gather_rows(up_weights, "ry", "rz")
    down_full_t = gather_rows(jnp.transpose(down_weights), "rz", "ry")
    projected = jnp.einsum(
        "nd,dhc->nhc", owner_slab, head_weights, preferred_element_type=jnp.float32
    ).astype(jnp.bfloat16)
    queries = jnp.moveaxis(projected[:, :, :head_dim], 1, 0)
    key_rows = jnp.moveaxis(projected[:, :, head_dim : 2 * head_dim], 1, 0)
    value_rows = jnp.moveaxis(projected[:, :, 2 * head_dim :], 1, 0)
    segment = segment_ids[0]
    position = jnp.arange(rows_all, dtype=jnp.int32)
    allowed = (position[:, None] >= position[None, :]) & (segment[:, None] == segment[None, :])
    scale = 1.0 / math.sqrt(head_dim)

    def one_head(operands):
        query_head, key_head, value_head = operands
        scores = (
            lax.dot_general(
                query_head, key_head, (((1,), (1,)), ((), ())), preferred_element_type=jnp.float32
            )
            * scale
        )
        scores = jnp.where(allowed, scores, -1e30)
        probs = jax.nn.softmax(scores, axis=-1).astype(jnp.bfloat16)
        return jnp.dot(probs, value_head, preferred_element_type=jnp.float32).astype(jnp.bfloat16)

    attended = jnp.moveaxis(lax.map(one_head, (queries, key_rows, value_rows)), 0, 1)
    own = lax.axis_index("grp")
    own_rows = lax.dynamic_slice_in_dim(owner_slab, own * quarter, quarter, 0).astype(jnp.float32)
    partial_rows = jnp.einsum(
        "nhd,hde->ne", attended, merge_weights, preferred_element_type=jnp.float32
    )
    mixed = lax.psum_scatter(partial_rows, "grp", scatter_dimension=0, tiled=True)
    hidden = layer_norm(own_rows + mixed, first_gain, first_bias).astype(jnp.bfloat16)
    slots = quarter // owners
    placed = jnp.zeros_like(hidden).at[row_map[0, 0]].set(hidden)
    staged = placed.reshape(zs, owners // zs, slots * width)
    staged = lax.all_to_all(staged, "rz", split_axis=0, concat_axis=0, tiled=True)
    staged = lax.all_to_all(staged, ("ry", "rc"), split_axis=1, concat_axis=1, tiled=True)
    even_rows = staged.reshape(quarter, width)
    group_rows = lax.all_gather(even_rows, "grp", axis=0, tiled=True)
    raised = jnp.dot(group_rows, up_full, preferred_element_type=jnp.float32)
    activated = jax.nn.gelu(raised, approximate=False).astype(jnp.bfloat16)
    lowered_all = lax.dot_general(
        activated, down_full_t, (((1,), (1,)), ((), ())), preferred_element_type=jnp.float32
    )
    lowered = lax.psum_scatter(lowered_all, "grp", scatter_dimension=0, tiled=True)
    layer_out = layer_norm(
        even_rows.astype(jnp.float32) + lowered, second_gain, second_bias
    ).astype(jnp.bfloat16)
    page_count = page_table.shape[1]
    page_rows = rows_all // page_count
    stacked = projected[:, :, head_dim:].reshape(page_count, page_rows, local_heads, 2 * head_dim)
    cache_pages = jnp.zeros_like(stacked).at[page_table[0]].set(stacked)
    return (layer_out, cache_pages)


def solution(mesh):
    zs, ys, cores = split_req(mesh)
    devices = np.asarray(mesh.devices).reshape(zs, ys, cores, mesh.devices.shape[1])
    inner = Mesh(devices, REQ + ("grp",))
    in_specs = (
        P(REQ, None),
        P(REQ, None),
        P(None, "grp", None),
        P("grp", None, None),
        P(),
        P(),
        P(REQ, "grp"),
        P("grp", REQ),
        P(),
        P(),
        P(REQ, None),
        P(REQ, "grp", None),
    )
    out_specs = (P(REQ + ("grp",), None), P(REQ, None, "grp", None))
    return jax.shard_map(local, mesh=inner, in_specs=in_specs, out_specs=out_specs, check_vma=False)
```

profile of v0, /device:TPU:1, one launch (start us, length us, event | category | flops | bytes accessed | tf_op | source)
XLA Modules:
  0.0 255.3 jit_solution(2603240170650563449)
XLA Ops:
  8.1 23.0 %all-gather = bf16[64,1024]{1,0:T(8,128)(2,1)} all-gather(bf16[8,1024]{1,0:T(8,128)(2,1)} %param.20), channel_id=2, replica_groups=mesh['rz'=8,'ry'=8,'rc'=2,'grp'=4] {'ry'}, dimensions={0}, use_global_device_ids=true | all-gather | bytes 147456 | tf_op jit(solution)/shard_map/all_gather | solution.py:33
  31.1 27.1 %all-gather.3 = bf16[64,1024]{1,0:T(8,128)(2,1)} all-gather(bf16[8,1024]{1,0:T(8,128)(2,1)} %bitcast.90), channel_id=5, replica_groups=mesh['rz'=8,'ry'=8,'rc'=2,'grp'=4] {'rz'}, dimensions={0}, use_global_device_ids=true | all-gather | bytes 147456 | tf_op jit(solution)/shard_map/all_gather | solution.py:33
  58.3 2.2 fusion.101
  60.7 0.5 copy-done.7
  61.2 3.7 %while.11 = (s32[]{:T(128)}, bf16[4,512,64]{1,2,0:T(8,128)(2,1)S(1)}, bf16[4,512,64]{1,2,0:T(8,128)(2,1)S(1)}, bf16[4,512,64]{1,2,0:T(8,128)(2,1)S(1)}, bf16[4,5...) while((s32[]{:T(128)}, bf16[4,512,64]{1,2,0:T(8,128)(2,1)S(1)}, ...), condition=%wide.region_3.4_spmd.clone, body=%wide.region_0.3_spmd.clone.sunk | while | flops 70024192 | bytes 3424341 | solution.py:90
  64.9 2.8 %convolution_bitcast_fusion = f32[512,1024]{1,0:T(8,128)} fusion(bf16[4,64,1024]{2,1,0:T(8,128)(2,1)} %param.17, bf16[4,512,64]{1,2,0:T(8,128)(2,1)S(1)} %get-tuple-element.34), kind=kOutput, calls=%fused_computation.40 | convolution fusion | flops 268435456 | bytes 2883584 | tf_op jit(solution)/shard_map/nhd,hde->ne/dot_general | solution.py:93
  67.9 10.0 %all-gather.14.cloned.1.call-done = bf16[64,8,1024]{2,1,0:T(8,128)(2,1)} async-done(((bf16[8,8,1024]{2,1,0:T(8,128)(2,1)}), bf16[64,8,1024]{2,1,0:T(8,128)(2,1)}) %all-gather.14.cloned.1.call-update) | async-done | bytes 1048592 | tf_op jit(solution)/shard_map/all_gather | solution.py:34
  78.0 41.6 %all-gather.18.cloned.1.call-done = bf16[64,8,1024]{2,1,0:T(8,128)(2,1)} async-done(((bf16[8,8,1024]{2,1,0:T(8,128)(2,1)}), bf16[64,8,1024]{2,1,0:T(8,128)(2,1)}) %all-gather.18.cloned.1.call-update) | async-done | bytes 1048592 | tf_op jit(solution)/shard_map/all_gather | solution.py:34
  119.7 1.2 fusion.64
  120.9 1.2 multiply_reduce_fusion.1
  122.2 1.9 scatter_custom_fusion
  124.1 16.0 %all_to_all.10 = bf16[8,16,1024]{2,1,0:T(8,128)(2,1)S(1)} all-to-all(bf16[8,16,1024]{2,1,0:T(8,128)(2,1)S(1)} %bitcast.87), channel_id=1, replica_groups=mesh['rz'=8,'ry'=8,'rc'=2,'grp'=4] {'rz'}, dimensions={0} | all-to-all | bytes 524288 | tf_op jit(solution)/shard_map/all_to_all | solution.py:101
  140.3 21.8 %all_to_all.11 = bf16[8,16,1024]{2,0,1:T(8,128)(2,1)S(1)} all-to-all(bf16[8,16,1024]{2,0,1:T(8,128)(2,1)S(1)} %copy.42), channel_id=1, replica_groups=mesh['rz'=8,'ry'=8,'rc'=2,'grp'=4] {'ry','rc'}, dimensions={1} | all-to-all | bytes 524288 | tf_op jit(solution)/shard_map/all_to_all | solution.py:102
  162.1 0.9 copy.43
  163.2 3.2 %copy.44 = bf16[8,8,2,8,1024]{4,3,2,1,0:T(8,128)(2,1)} copy(bf16[8,8,2,8,1024]{4,3,1,0,2:T(8,128)(2,1)} %bitcast.80) | data formatting | bytes 4194304 | tf_op jit(solution)/shard_map/transpose | solution.py:37
  166.5 3.1 %copy.45 = bf16[8,8,2,8,1024]{4,3,2,1,0:T(8,128)(2,1)} copy(bf16[8,8,2,8,1024]{4,3,0,1,2:T(8,128)(2,1)} %bitcast.81) | data formatting | bytes 4194304 | tf_op jit(solution)/shard_map/transpose | solution.py:39
  169.6 26.6 %all-gather.12.cloned.1.call-done = bf16[512,1024]{1,0:T(8,128)(2,1)} async-done(((bf16[128,1024]{1,0:T(8,128)(2,1)}), bf16[512,1024]{1,0:T(8,128)(2,1)}) %all-gather.12.cloned.1.call-update) | async-done | bytes 1048592 | tf_op jit(solution)/shard_map/all_gather | solution.py:104
  196.3 10.1 %fusion.25 = f32[512,1024]{1,0:T(8,128)} fusion(bf16[1024,1024]{1,0:T(8,128)(2,1)} %bitcast.83, bf16[512,1024]{1,0:T(8,128)(2,1)} %all-gather.12.cloned.1.call-done, bf16[1024,1024]{1,0:T(8,128)(2,1)} %bitcast.82), kind=kOutput, calls=%fused_computation.41 | convolution fusion | flops 2181562368 | bytes 7340032 | tf_op jit(solution)/shard_map/dot_general | solution.py:107
  207.2 0.8 scatter_fusion
  208.0 1.2 copy.47
  209.2 34.7 %reduce-scatter.5.cloned.1.call-done = f32[128,1024]{1,0:T(8,128)} async-done(((f32[512,1024]{1,0:T(8,128)}), f32[128,1024]{1,0:T(8,128)}) %reduce-scatter.5.cloned.1.call-update) | async-done | bytes 524304 | tf_op jit(solution)/shard_map/reduce_scatter | solution.py:110
  243.9 1.2 fusion.63
  245.0 1.2 multiply_reduce_fusion
  246.3 1.9 add_convert_fusion
  (62 shorter events, 5.6 us)
Async XLA Ops:
  8.0 50.3 %copy-start = (bf16[1024,4,192]{0,2,1:T(8,128)(2,1)S(1)}, bf16[1024,4,192]{0,2,1:T(8,128)(2,1)}, u32[]{:S(2)}) copy-start(bf16[1024,4,192]{0,2,1:T(8,128)(2,1)} %param.16) | copy-start | bytes 4718596
  8.0 69.9 %all-gather.14.cloned.1.call-start = ((), (), s32[]{:S(2)}) async-start(), calls=%async_computation.7 | async-start | bytes 1179648 | tf_op jit(solution)/shard_map/all_gather | solution.py:34
  31.1 88.5 %all-gather.18.cloned.1.call-start = ((), (), s32[]{:S(2)}) async-start(), calls=%async_computation.9 | async-start | bytes 1179648 | tf_op jit(solution)/shard_map/all_gather | solution.py:34
  58.2 61.5 %reduce-scatter.3.cloned.1.call-start = ((), (), s32[]{:S(2)}) async-start(), calls=%async_computation.4 | async-start | bytes 2621440 | tf_op jit(solution)/shard_map/reduce_scatter | solution.py:96
  60.5 0.7 copy-start.7
  67.8 51.9 %copy-start.8 = (s32[1,1,128]{2,1,0:T(1,128)S(1)}, s32[1,1,128]{2,1,0:T(1,128)}, u32[]{:S(2)}) copy-start(s32[1,1,128]{2,1,0:T(1,128)} %param.25) | copy-start | bytes 1540
  67.8 51.9 %copy-start.2 = (bf16[512,1024]{1,0:T(8,128)(2,1)S(1)}, bf16[512,1024]{1,0:T(8,128)(2,1)}, u32[]{:S(2)}) copy-start(bf16[512,1024]{1,0:T(8,128)(2,1)} %param.14) | copy-start | bytes 3145732
  67.8 54.4 %copy-start.3 = (f32[1024]{0:T(1024)S(1)}, f32[1024]{0:T(1024)}, u32[]{:S(2)}) copy-start(f32[1024]{0:T(1024)} %param.19) | copy-start | bytes 12292
  67.8 54.4 %copy-start.4 = (f32[1024]{0:T(1024)S(1)}, f32[1024]{0:T(1024)}, u32[]{:S(2)}) copy-start(f32[1024]{0:T(1024)} %param.18) | copy-start | bytes 12292
  67.8 95.4 %all-gather.16.cloned.1.call-start = ((), (), s32[]{:S(2)}) async-start(), calls=%async_computation.8 | async-start | bytes 3145728 | tf_op jit(solution)/shard_map/all_gather | solution.py:35
  78.0 88.5 %all-gather.20.cloned.1.call-start = ((), (), s32[]{:S(2)}) async-start(), calls=%async_computation.10 | async-start | bytes 3145728 | tf_op jit(solution)/shard_map/all_gather | solution.py:35
  119.6 76.6 %all-gather.12.cloned.1.call-start = ((), (), s32[]{:S(2)}) async-start(), calls=%async_computation.5 | async-start | bytes 1310720 | tf_op jit(solution)/shard_map/all_gather | solution.py:104
  162.9 80.9 %reduce-scatter.5.cloned.1.call-start = ((), (), s32[]{:S(2)}) async-start(), calls=%async_computation.6 | async-start | bytes 2621440 | tf_op jit(solution)/shard_map/reduce_scatter | solution.py:110
  206.4 0.7 copy-start.9
  206.6 37.3 %copy-start.1 = (bf16[8,16,1024]{2,1,0:T(8,128)(2,1)S(1)}, bf16[8,16,1024]{2,1,0:T(8,128)(2,1)}, u32[]{:S(2)}) copy-start(bf16[8,16,1024]{2,1,0:T(8,128)(2,1)} %copy.43) | copy-start | bytes 786436
  207.2 39.1 %copy-start.5 = (f32[1024]{0:T(1024)S(1)}, f32[1024]{0:T(1024)}, u32[]{:S(2)}) copy-start(f32[1024]{0:T(1024)} %param.23) | copy-start | bytes 12292
  207.2 39.1 %copy-start.6 = (f32[1024]{0:T(1024)S(1)}, f32[1024]{0:T(1024)}, u32[]{:S(2)}) copy-start(f32[1024]{0:T(1024)} %param.22) | copy-start | bytes 12292
Sparse Core Ops, SparseCore 0:
  31.2 46.7 all-gather.13
  80.0 39.5 all-gather.17
  121.7 22.7 all-gather.15
  146.4 20.0 all-gather.19
  169.0 27.1 all-gather.11
Sparse Core Ops, SparseCore 1:
  67.9 44.0 reduce-scatter.2
  206.5 37.3 reduce-scatter.4
where the time goes:
time: 256 us; the launch traced here: 255 us
  waiting for transfers between devices  113 us (44%)
  blocking collectives  87.8 us (34%)
  matrix products  18.1 us (7%)
  between operations  15.5 us (6%)
  local copies, waits for them, and re-layouts  10.6 us (4%)
  other arithmetic  9.59 us (4%)
    all_gather x2, waiting for transfers between devices, gather_rows(): b = lax.all_gather(a, second, axis=0, tiled=False)  51.6 us
    all_gather x2, blocking collectives, gather_rows(): a = lax.all_gather(block, first, axis=0, tiled=False)  50 us
    reduce_scatter x1, waiting for transfers between devices, local(): lax.psum_scatter(lowered_all, 'grp', scatter_dimension=0, tiled=True)  34.7 us
    all_gather x1, waiting for transfers between devices, local(): group_rows = lax.all_gather(even_rows, 'grp', axis=0, tiled=True)  26.6 us
    all_to_all x1, blocking collectives, local(): lax.all_to_all(staged, ('ry', 'rc'), split_axis=1, concat_axis=1, tiled=T...  21.8 us
    all_to_all x1, blocking collectives, local(): lax.all_to_all(staged, 'rz', split_axis=0, concat_axis=0, tiled=True)  16 us
    dot_general x1, matrix products, local(): lax.dot_general(activated, down_full_t, (((1,), (1,)), ((), ())), preferr...  10.1 us
  transfers between devices with their start and end apart: 7, of which 5 were waited for; matrix products, arithmetic and copies ran while one was open for 9% of the time, Pallas kernels for 0%

commit v1 on v0

--- a/solution.py
+++ b/solution.py
@@ -8,6 +8,12 @@
 
 EPSILON = 1e-05
 REQ = ("rz", "ry", "rc")
+
+
+def in_order(blocks, dim):
+    blocks = jnp.moveaxis(blocks, 0, dim)
+    shape = blocks.shape
+    return blocks.reshape(*shape[:dim], shape[dim] * shape[dim + 1], *shape[dim + 2 :])
 
 
 def layer_norm(values, gain, bias):
@@ -101,7 +107,19 @@
     staged = lax.all_to_all(staged, "rz", split_axis=0, concat_axis=0, tiled=True)
     staged = lax.all_to_all(staged, ("ry", "rc"), split_axis=1, concat_axis=1, tiled=True)
     even_rows = staged.reshape(quarter, width)
-    group_rows = lax.all_gather(even_rows, "grp", axis=0, tiled=True)
+    length = lax.axis_size("grp")
+    pairs = [(i, (i + 1) % length) for i in range(length)]
+    back = [(b_2, a_2) for a_2, b_2 in pairs]
+    lower, upper = ([], [])
+    for step in range(length - 1):
+        if step % 2 == 0:
+            lower.append(lax.ppermute(lower[-1] if lower else even_rows, "grp", pairs))
+        else:
+            upper.append(lax.ppermute(upper[-1] if upper else even_rows, "grp", back))
+    blocks = jnp.stack([*lower[::-1], even_rows, *upper])
+    shift = lax.axis_index("grp") - len(lower)
+    blocks = blocks[(jnp.arange(length) - shift) % length]
+    group_rows = in_order(blocks, 0)
     raised = jnp.dot(group_rows, up_full, preferred_element_type=jnp.float32)
     activated = jax.nn.gelu(raised, approximate=False).astype(jnp.bfloat16)
     lowered_all = lax.dot_general(

time: 256 us -> 235 us (0.918)
  waiting for transfers between devices: 113 us -> 80.5 us
  starting transfers between devices: 0.46 us -> 8.83 us
    all_gather x1 -> x0, waiting for transfers between devices: 26.6 us -> none  [local(): group_rows = lax.all_gather(even_rows, 'grp', axis=0, tiled=True)]
    reduce_scatter x1, waiting for transfers between devices: 34.7 us -> 22 us  [local(): lax.psum_scatter(lowered_all, 'grp', scatter_dimension=0, tiled=True)]
    ppermute x0 -> x3, starting transfers between devices: none -> 8.58 us  [the longest x2 5.14 us: local(): lower.append(lax.ppermute(lower[-1] if lower else even_rows, 'grp', pairs))]
    ppermute x0 -> x3, waiting for transfers between devices: none -> 6.75 us  [the longest x2 6.74 us: local(): lower.append(lax.ppermute(lower[-1] if lower else even_rows, 'grp', pairs))]
    gather x0 -> x1, local copies, waits for them, and re-layouts: none -> 2.83 us  [local(): blocks = blocks[(jnp.arange(length) - shift) % length]]
  transfers between devices with their start and end apart: 7 -> 9, of which waited for: 5 -> 5; matrix products, arithmetic and copies ran while one was open for 9% -> 10% of each run, Pallas kernels for 0% -> 0%
where the time goes in v1:
time: 235 us; the launch traced here: 234 us
  blocking collectives  87.8 us (37%)
  waiting for transfers between devices  80.5 us (34%)
  matrix products  18.1 us (8%)
  between operations  15.5 us (7%)
  local copies, waits for them, and re-layouts  12.8 us (5%)
  other arithmetic  10.7 us (5%)
  starting transfers between devices  8.83 us (4%)
    all_gather x2, waiting for transfers between devices, gather_rows(): b = lax.all_gather(a, second, axis=0, tiled=False)  51.6 us
    all_gather x2, blocking collectives, gather_rows(): a = lax.all_gather(block, first, axis=0, tiled=False)  50 us
    reduce_scatter x1, waiting for transfers between devices, local(): lax.psum_scatter(lowered_all, 'grp', scatter_dimension=0, tiled=True)  22 us
    all_to_all x1, blocking collectives, local(): lax.all_to_all(staged, ('ry', 'rc'), split_axis=1, concat_axis=1, tiled=T...  21.8 us
    all_to_all x1, blocking collectives, local(): lax.all_to_all(staged, 'rz', split_axis=0, concat_axis=0, tiled=True)  16 us
    dot_general x1, matrix products, local(): lax.dot_general(activated, down_full_t, (((1,), (1,)), ((), ())), preferr...  10.1 us
    ppermute x2, waiting for transfers between devices, local(): lower.append(lax.ppermute(lower[-1] if lower else even_rows, 'grp', pairs))  6.74 us
    ppermute x2, starting transfers between devices, local(): lower.append(lax.ppermute(lower[-1] if lower else even_rows, 'grp', pairs))  5.14 us
  transfers between devices with their start and end apart: 9, of which 5 were waited for; matrix products, arithmetic and copies ran while one was open for 10% of the time, Pallas kernels for 0%

profile of v1, /device:TPU:1, one launch (start us, length us, event | category | flops | bytes accessed | tf_op | source)
XLA Modules:
  0.0 234.2 jit_solution(345942135970446218)
XLA Ops:
  8.1 23.0 %all-gather = bf16[64,1024]{1,0:T(8,128)(2,1)} all-gather(bf16[8,1024]{1,0:T(8,128)(2,1)} %param.20), channel_id=2, replica_groups=mesh['rz'=8,'ry'=8,'rc'=2,'grp'=4] {'ry'}, dimensions={0}, use_global_device_ids=true | all-gather | bytes 147456 | tf_op jit(solution)/shard_map/all_gather | solution.py:39
  31.1 27.1 %all-gather.3 = bf16[64,1024]{1,0:T(8,128)(2,1)} all-gather(bf16[8,1024]{1,0:T(8,128)(2,1)} %bitcast.103), channel_id=5, replica_groups=mesh['rz'=8,'ry'=8,'rc'=2,'grp'=4] {'rz'}, dimensions={0}, use_global_device_ids=true | all-gather | bytes 147456 | tf_op jit(solution)/shard_map/all_gather | solution.py:39
  58.3 2.2 fusion.103
  61.2 3.7 %while.11 = (s32[]{:T(128)}, bf16[4,512,64]{1,2,0:T(8,128)(2,1)S(1)}, bf16[4,512,64]{1,2,0:T(8,128)(2,1)S(1)}, bf16[4,512,64]{1,2,0:T(8,128)(2,1)S(1)}, bf16[4,5...) while((s32[]{:T(128)}, bf16[4,512,64]{1,2,0:T(8,128)(2,1)S(1)}, ...), condition=%wide.region_3.4_spmd.clone, body=%wide.region_0.3_spmd.clone.sunk | while | flops 70024192 | bytes 3424341 | solution.py:96
  64.9 2.9 %convolution_bitcast_fusion = f32[512,1024]{1,0:T(8,128)} fusion(bf16[4,64,1024]{2,1,0:T(8,128)(2,1)} %param.17, bf16[4,512,64]{1,2,0:T(8,128)(2,1)S(1)} %get-tuple-element.34), kind=kOutput, calls=%fused_computation.41 | convolution fusion | flops 268435456 | bytes 2883584 | tf_op jit(solution)/shard_map/nhd,hde->ne/dot_general | solution.py:99
  67.9 10.0 %all-gather.11.cloned.1.call-done = bf16[64,8,1024]{2,1,0:T(8,128)(2,1)} async-done(((bf16[8,8,1024]{2,1,0:T(8,128)(2,1)}), bf16[64,8,1024]{2,1,0:T(8,128)(2,1)}) %all-gather.11.cloned.1.call-update) | async-done | bytes 1048592 | tf_op jit(solution)/shard_map/all_gather | solution.py:40
  78.0 41.6 %all-gather.15.cloned.1.call-done = bf16[64,8,1024]{2,1,0:T(8,128)(2,1)} async-done(((bf16[8,8,1024]{2,1,0:T(8,128)(2,1)}), bf16[64,8,1024]{2,1,0:T(8,128)(2,1)}) %all-gather.15.cloned.1.call-update) | async-done | bytes 1048592 | tf_op jit(solution)/shard_map/all_gather | solution.py:40
  120.9 1.2 multiply_reduce_fusion.1
  122.2 1.9 scatter_custom_fusion
  124.1 16.0 %all_to_all.10 = bf16[8,16,1024]{2,1,0:T(8,128)(2,1)S(1)} all-to-all(bf16[8,16,1024]{2,1,0:T(8,128)(2,1)S(1)} %bitcast.97), channel_id=1, replica_groups=mesh['rz'=8,'ry'=8,'rc'=2,'grp'=4] {'rz'}, dimensions={0} | all-to-all | bytes 524288 | tf_op jit(solution)/shard_map/all_to_all | solution.py:107
  140.3 21.8 %all_to_all.11 = bf16[8,16,1024]{2,0,1:T(8,128)(2,1)S(1)} all-to-all(bf16[8,16,1024]{2,0,1:T(8,128)(2,1)S(1)} %copy.43), channel_id=1, replica_groups=mesh['rz'=8,'ry'=8,'rc'=2,'grp'=4] {'ry','rc'}, dimensions={1} | all-to-all | bytes 524288 | tf_op jit(solution)/shard_map/all_to_all | solution.py:108
  162.2 3.0 %collective-permute-start = (bf16[128,1024]{1,0:T(8,128)(2,1)S(1)}, bf16[128,1024]{1,0:T(8,128)(2,1)S(1)}, u32[]{:S(2)}, u32[]{:S(2)}) collective-permute-start(bf16[128,1024]{1,0:T(8,128)(2,1)S(1)} %bitcast.86), channel_id=1, source_target_pairs={{0,1},{1,2},{2,3},{3,0},{4,5},{5,6},{6,7},{7,4},{8,9},{9,10},{10,1... | collective-permute-start | bytes 786440 | tf_op jit(solution)/shard_map/ppermute | solution.py:116
  165.3 3.4 %collective-permute-start.2 = (bf16[128,1024]{1,0:T(8,128)(2,1)S(1)}, bf16[128,1024]{1,0:T(8,128)(2,1)S(1)}, u32[]{:S(2)}, u32[]{:S(2)}) collective-permute-start(bf16[128,1024]{1,0:T(8,128)(2,1)S(1)} %bitcast.87), channel_id=1, source_target_pairs={{1,0},{2,1},{3,2},{0,3},{5,4},{6,5},{7,6},{4,7},{9,8},{10,9},{11,1... | collective-permute-start | bytes 786440 | tf_op jit(solution)/shard_map/ppermute | solution.py:118
  168.7 4.8 %collective-permute-done = bf16[128,1024]{1,0:T(8,128)(2,1)S(1)} collective-permute-done((bf16[128,1024]{1,0:T(8,128)(2,1)S(1)}, bf16[128,1024]{1,0:T(8,128)(2,1)S(1)}, u32[]{:S(2)}, u32[]{:S(2)}) %collective-permute-start) | collective-permute-done | bytes 262176 | tf_op jit(solution)/shard_map/ppermute | solution.py:116
  173.5 2.1 collective-permute-start.1
  175.7 3.2 %copy.46 = bf16[8,8,2,8,1024]{4,3,2,1,0:T(8,128)(2,1)} copy(bf16[8,8,2,8,1024]{4,3,1,0,2:T(8,128)(2,1)} %bitcast.89) | data formatting | bytes 4194304 | tf_op jit(solution)/shard_map/transpose | solution.py:43
  178.8 3.2 %copy.47 = bf16[8,8,2,8,1024]{4,3,2,1,0:T(8,128)(2,1)} copy(bf16[8,8,2,8,1024]{4,3,0,1,2:T(8,128)(2,1)} %bitcast.90) | data formatting | bytes 4194304 | tf_op jit(solution)/shard_map/transpose | solution.py:45
  182.0 1.9 collective-permute-done.1
  185.1 2.8 %gather_fusion = bf16[4,128,1024]{2,1,0:T(8,128)(2,1)} fusion(bf16[4,128,1024]{2,1,0:T(8,128)(2,1)} %pad_maximum_fusion, s32[1024]{0:T(1024)S(1)} %pad_clamp_fusion), kind=kCustom, calls=%fused_computation | custom fusion | bytes 2097168 | tf_op jit(solution)/shard_map/gather | solution.py:121
  187.9 10.1 %fusion.25 = f32[512,1024]{1,0:T(8,128)} fusion(bf16[1024,1024]{1,0:T(8,128)(2,1)} %bitcast.92, bf16[512,1024]{1,0:T(8,128)(2,1)} %bitcast.94, bf16[1024,1024]{1,0:T(8,128)(2,1)} %bitcast.91), kind=kOutput, calls=%fused_computation.42 | convolution fusion | flops 2181562368 | bytes 7340032 | tf_op jit(solution)/shard_map/dot_general | solution.py:125
  199.5 1.2 copy.49
  200.8 22.0 %reduce-scatter.5.cloned.1.call-done = f32[128,1024]{1,0:T(8,128)} async-done(((f32[512,1024]{1,0:T(8,128)}), f32[128,1024]{1,0:T(8,128)}) %reduce-scatter.5.cloned.1.call-update) | async-done | bytes 524304 | tf_op jit(solution)/shard_map/reduce_scatter | solution.py:128
  223.9 1.2 multiply_reduce_fusion
  225.2 1.9 add_convert_fusion
  (67 shorter events, 10.1 us)
Async XLA Ops:
  8.0 50.3 %copy-start = (bf16[1024,4,192]{0,2,1:T(8,128)(2,1)S(1)}, bf16[1024,4,192]{0,2,1:T(8,128)(2,1)}, u32[]{:S(2)}) copy-start(bf16[1024,4,192]{0,2,1:T(8,128)(2,1)} %param.16) | copy-start | bytes 4718596
  8.0 69.9 %all-gather.11.cloned.1.call-start = ((), (), s32[]{:S(2)}) async-start(), calls=%async_computation.6 | async-start | bytes 1179648 | tf_op jit(solution)/shard_map/all_gather | solution.py:40
  31.1 88.5 %all-gather.15.cloned.1.call-start = ((), (), s32[]{:S(2)}) async-start(), calls=%async_computation.8 | async-start | bytes 1179648 | tf_op jit(solution)/shard_map/all_gather | solution.py:40
  58.2 61.5 %reduce-scatter.3.cloned.1.call-start = ((), (), s32[]{:S(2)}) async-start(), calls=%async_computation.4 | async-start | bytes 2621440 | tf_op jit(solution)/shard_map/reduce_scatter | solution.py:102
  60.5 0.7 copy-start.6
  67.8 10.2 %copy-start.7 = (s32[1,1,128]{2,1,0:T(1,128)S(1)}, s32[1,1,128]{2,1,0:T(1,128)}, u32[]{:S(2)}) copy-start(s32[1,1,128]{2,1,0:T(1,128)} %param.25) | copy-start | bytes 1540
  67.8 51.9 %copy-start.1 = (bf16[512,1024]{1,0:T(8,128)(2,1)S(1)}, bf16[512,1024]{1,0:T(8,128)(2,1)}, u32[]{:S(2)}) copy-start(bf16[512,1024]{1,0:T(8,128)(2,1)} %param.14) | copy-start | bytes 3145732
  67.8 54.3 %copy-start.2 = (f32[1024]{0:T(1024)S(1)}, f32[1024]{0:T(1024)}, u32[]{:S(2)}) copy-start(f32[1024]{0:T(1024)} %param.19) | copy-start | bytes 12292
  67.9 54.3 %copy-start.3 = (f32[1024]{0:T(1024)S(1)}, f32[1024]{0:T(1024)}, u32[]{:S(2)}) copy-start(f32[1024]{0:T(1024)} %param.18) | copy-start | bytes 12292
  67.9 107.8 %all-gather.13.cloned.1.call-start = ((), (), s32[]{:S(2)}) async-start(), calls=%async_computation.7 | async-start | bytes 3145728 | tf_op jit(solution)/shard_map/all_gather | solution.py:41
  78.0 100.9 %all-gather.17.cloned.1.call-start = ((), (), s32[]{:S(2)}) async-start(), calls=%async_computation.9 | async-start | bytes 3145728 | tf_op jit(solution)/shard_map/all_gather | solution.py:41
  119.6 103.1 %reduce-scatter.5.cloned.1.call-start = ((), (), s32[]{:S(2)}) async-start(), calls=%async_computation.5 | async-start | bytes 2621440 | tf_op jit(solution)/shard_map/reduce_scatter | solution.py:128
  162.2 11.3 %collective-permute-start = (bf16[128,1024]{1,0:T(8,128)(2,1)S(1)}, bf16[128,1024]{1,0:T(8,128)(2,1)S(1)}, u32[]{:S(2)}, u32[]{:S(2)}) collective-permute-start(bf16[128,1024]{1,0:T(8,128)(2,1)S(1)} %bitcast.86), channel_id=1, source_target_pairs={{0,1},{1,2},{2,3},{3,0},{4,5},{5,6},{6,7},{7,4},{8,9},{9,10},{10,1... | collective-permute-start | bytes 786440 | tf_op jit(solution)/shard_map/ppermute | solution.py:116
  165.3 16.8 %collective-permute-start.2 = (bf16[128,1024]{1,0:T(8,128)(2,1)S(1)}, bf16[128,1024]{1,0:T(8,128)(2,1)S(1)}, u32[]{:S(2)}, u32[]{:S(2)}) collective-permute-start(bf16[128,1024]{1,0:T(8,128)(2,1)S(1)} %bitcast.87), channel_id=1, source_target_pairs={{1,0},{2,1},{3,2},{0,3},{5,4},{6,5},{7,6},{4,7},{9,8},{10,9},{11,1... | collective-permute-start | bytes 786440 | tf_op jit(solution)/shard_map/ppermute | solution.py:118
  173.5 10.4 %collective-permute-start.1 = (bf16[128,1024]{1,0:T(8,128)(2,1)S(1)}, bf16[128,1024]{1,0:T(8,128)(2,1)S(1)}, u32[]{:S(2)}, u32[]{:S(2)}) collective-permute-start(bf16[128,1024]{1,0:T(8,128)(2,1)S(1)} %collective-permute-done), channel_id=1, source_target_pairs={{0,1},{1,2},{2,3},{3,0},{4,5},{5,6},{6,7},{7,4},{8,9},{9,10},{10,1... | collective-permute-start | bytes 786440 | tf_op jit(solution)/shard_map/ppermute | solution.py:116
  198.0 0.7 copy-start.8
  198.7 26.4 %copy-start.4 = (f32[1024]{0:T(1024)S(1)}, f32[1024]{0:T(1024)}, u32[]{:S(2)}) copy-start(f32[1024]{0:T(1024)} %param.23) | copy-start | bytes 12292
  198.8 26.4 %copy-start.5 = (f32[1024]{0:T(1024)S(1)}, f32[1024]{0:T(1024)}, u32[]{:S(2)}) copy-start(f32[1024]{0:T(1024)} %param.22) | copy-start | bytes 12292
Sparse Core Ops, SparseCore 0:
  31.2 46.7 all-gather.10
  80.0 39.5 all-gather.14
  121.7 22.7 all-gather.12
  146.4 20.0 all-gather.16
Sparse Core Ops, SparseCore 1:
  67.9 44.0 reduce-scatter.2
  198.1 24.6 reduce-scatter.4
